TPU v7x, 32 devices: a whole 2x2x4 slice. The times are simulated.
32 devices in a mesh: space: 4 (over y, core), energy: 8 (over z, x).
Axes of the slice: x: 2, y: 2, z: 4, core: 2. Of those that a mesh axis runs over, the one named last changes fastest.
Arguments:
- lesser: bfloat16 [8, 4, 3, 128, 256], P('energy', 'space'), may hold values from -6 to 6
- greater: bfloat16 [8, 4, 3, 128, 256], P('energy', 'space'), may hold values from -2.109375 to 2.109375
Outputs:
- polarization: float32 [8, 4, 3, 128, 256], P('energy', 'space')
All inputs are finite; a program needn't handle non-finite values.
Results may differ from a plain program's by a relative error of at most 0.0003.
Values may be sent and summed in bfloat16 or wider, within the bound.
No kernel may reach another device: no remote copies, remote signals or barrier semaphores. Data moves between devices by JAX's collectives and lax.ppermute only.
A program may use at most 64 MiB of HBM per device.

v0:
```python
import math

import jax
import jax.numpy as jnp
from jax import lax
from jax.sharding import PartitionSpec as P


def with_halo(block, sides, width):
    for axis, dim in sides:
        count = lax.axis_size(axis)
        forward = [(i, i + 1) for i in range(count - 1)]
        backward = [(target, source) for source, target in forward]
        low = lax.ppermute(
            lax.slice_in_dim(block, block.shape[dim] - width, None, axis=dim), axis, forward
        )
        high = lax.ppermute(lax.slice_in_dim(block, 0, width, axis=dim), axis, backward)
        block = jnp.concatenate([low, block, high], axis=dim)
    return block


def flip_tiles(tiles):
    shape = tiles.shape
    width = shape[-2]
    split = tiles.reshape(shape[:-1] + (2, width))
    turned = jnp.swapaxes(split, -3, -1)
    return turned.reshape(shape)


def correlate_rows(pair):
    left, right = pair
    total = left.shape[0]
    inner = left.shape[1:-1]
    width = left.shape[-1] // 2
    left = left.astype(jnp.float32).reshape((total, -1, 2, width))
    right = right.astype(jnp.float32).reshape((total, -1, 2, width))
    left_re = left[:, :, 0].reshape((total, -1))
    left_im = left[:, :, 1].reshape((total, -1))
    right_re = right[:, :, 0].reshape((total, -1))
    right_im = right[:, :, 1].reshape((total, -1))
    freq = lax.broadcasted_iota(jnp.int32, (total, total), 0)
    point = lax.broadcasted_iota(jnp.int32, (total, total), 1)
    phase = (freq * point % total).astype(jnp.float32) * (2.0 * math.pi / total)
    cosine = jnp.cos(phase)
    sine = jnp.sin(phase)
    high = lax.Precision.HIGHEST

    def apply(matrix, data):
        return jnp.dot(matrix, data, precision=high, preferred_element_type=jnp.float32)

    lhat_re = apply(cosine, left_re) + apply(sine, left_im)
    lhat_im = apply(cosine, left_im) - apply(sine, left_re)
    ghat_re = apply(cosine, right_re) - apply(sine, right_im)
    ghat_im = apply(cosine, right_im) + apply(sine, right_re)
    prod_re = lhat_re * ghat_re - lhat_im * ghat_im
    prod_im = lhat_re * ghat_im + lhat_im * ghat_re
    out_re = (apply(cosine.T, prod_re) - apply(sine.T, prod_im)) / total
    out_im = (apply(cosine.T, prod_im) + apply(sine.T, prod_re)) / total
    result = jnp.concatenate(
        [out_re.reshape((total,) + inner + (width,)), out_im.reshape((total,) + inner + (width,))],
        axis=-1,
    )
    return lax.all_to_all(result, "energy", split_axis=0, concat_axis=2, tiled=True)


def on_device(lesser, greater):
    own_lesser = lesser[:, 0]
    own_greater = greater[:, 0]
    rims = jnp.stack([own_greater[:, 0], own_greater[:, 2]], axis=1)
    padded = with_halo(rims, (("space", 1),), 1)
    mirrored = flip_tiles(jnp.stack([padded[:, 0], own_greater[:, 1], padded[:, 3]], axis=1))
    summed = correlate_rows(
        (
            lax.all_to_all(own_lesser, "energy", split_axis=2, concat_axis=0, tiled=True),
            lax.all_to_all(mirrored, "energy", split_axis=2, concat_axis=0, tiled=True),
        )
    )
    return summed[:, None]


def solution(mesh):
    return jax.shard_map(
        on_device,
        mesh=mesh,
        in_specs=(P("energy", "space", None, None, None), P("energy", "space", None, None, None)),
        out_specs=P("energy", "space", None, None, None),
        check_vma=False,
    )
```

profile of v0, /device:TPU:0, one launch (start us, length us, event | category | flops | bytes accessed | tf_op | source)
XLA Modules:
  0.0 53.7 jit_solution(16524863574397195299)
XLA Ops:
  0.0 1.8 %copy.72 = bf16[1,1,3,128,256]{4,2,3,1,0:T(4,128)(2,1)} copy(bf16[1,1,3,128,256]{4,3,2,1,0:T(8,128)(2,1)} %param.2) | data formatting | bytes 393216 | tf_op args[0]
  1.8 7.4 %all-to-all-start = ((bf16[1,3,128,256]{3,1,0,2:T(4,128)(2,1)}), bf16[1,3,128,256]{3,1,0,2:T(4,128)(2,1)S(1)}, u32[]{:S(2)}, u32[]{:S(2)}) async-start(bf16[1,3,128,256]{3,1,0,2:T(4,128)(2,1)} %bitcast.58), calls=%async_computation | async-start | bytes 524288 | tf_op jit(solution)/shard_map/all_to_all | solution.py:74
  9.4 1.5 %collective-permute-start = (bf16[1,1,128,256]{2,3,1,0:T(8,128)(2,1)S(1)}, bf16[1,1,128,256]{2,3,1,0:T(8,128)(2,1)S(1)}, u32[]{:S(2)}, u32[]{:S(2)}) collective-permute-start(bf16[1,1,128,256]{2,3,1,0:T(8,128)(2,1)S(1)} %get-tuple-element.11), channel_id=1, source_target_pairs={{0,8},{8,16},{16,24},{1,9},{9,17},{17,25},{2,10},{10,18},{18,26},{... | collective-permute-start | bytes 196616 | tf_op jit(solution)/shard_map/ppermute | solution.py:14
  10.9 1.3 %collective-permute-start.1 = (bf16[1,1,128,256]{2,3,1,0:T(8,128)(2,1)S(1)}, bf16[1,1,128,256]{2,3,1,0:T(8,128)(2,1)S(1)}, u32[]{:S(2)}, u32[]{:S(2)}) collective-permute-start(bf16[1,1,128,256]{2,3,1,0:T(8,128)(2,1)S(1)} %get-tuple-element.12), channel_id=1, source_target_pairs={{8,0},{16,8},{24,16},{9,1},{17,9},{25,17},{10,2},{18,10},{26,18},{... | collective-permute-start | bytes 196616 | tf_op jit(solution)/shard_map/ppermute | solution.py:17
  12.2 3.4 %collective-permute-done.1 = bf16[1,1,128,256]{2,3,1,0:T(8,128)(2,1)S(1)} collective-permute-done((bf16[1,1,128,256]{2,3,1,0:T(8,128)(2,1)S(1)}, bf16[1,1,128,256]{2,3,1,0:T(8,128)(2,1)S(1)}, u32[]{:S(2)}, u32[]{:S(2)}) %collective-permute-start.1) | collective-permute-done | bytes 65568 | tf_op jit(solution)/shard_map/ppermute | solution.py:17
  15.8 0.9 %copy.26 = bf16[1,3,128,256]{3,1,0,2:T(4,128)(2,1)} copy(bf16[1,3,128,256]{2,3,1,0:T(8,128)(2,1)S(1)} %bitcast.69) | data formatting | bytes 393216 | tf_op jit(solution)/shard_map/reshape | solution.py:27
  16.7 1.4 %all-to-all-done = bf16[1,3,128,256]{3,1,0,2:T(4,128)(2,1)S(1)} async-done(((bf16[1,3,128,256]{3,1,0,2:T(4,128)(2,1)}), bf16[1,3,128,256]{3,1,0,2:T(4,128)(2,1)S(1)}, u32[]{:S(2)}, u32[]{:S(2)}) %all-to-all-start) | async-done | bytes 196640 | tf_op jit(solution)/shard_map/all_to_all | solution.py:74
  18.1 4.6 %all-to-all-start.1 = ((bf16[1,3,128,256]{3,1,0,2:T(4,128)(2,1)}), bf16[1,3,128,256]{3,1,0,2:T(4,128)(2,1)S(1)}, u32[]{:S(2)}, u32[]{:S(2)}) async-start(bf16[1,3,128,256]{3,1,0,2:T(4,128)(2,1)} %copy.26), calls=%async_computation.1 | async-start | bytes 524288 | tf_op jit(solution)/shard_map/all_to_all | solution.py:75
  22.8 1.0 %slice_reduce_fusion.3 = (bf16[8,48,128]{2,1,0:T(8,128)(2,1)S(1)}, bf16[8,48,128]{2,1,0:T(8,128)(2,1)S(1)}) fusion(bf16[8,48,2,128]{3,2,1,0:T(2,128)(2,1)S(1)} %reshape.21), kind=kLoop, calls=%fused_computation.13 | loop fusion | bytes 393216 | tf_op jit(solution)/shard_map/slice | solution.py:37
  23.8 0.3 fusion.8
  24.1 0.3 fusion.12
  24.4 0.3 convolution_add_fusion.2
  24.7 6.4 %all-to-all-done.1 = bf16[1,3,128,256]{3,1,0,2:T(4,128)(2,1)S(1)} async-done(((bf16[1,3,128,256]{3,1,0,2:T(4,128)(2,1)}), bf16[1,3,128,256]{3,1,0,2:T(4,128)(2,1)S(1)}, u32[]{:S(2)}, u32[]{:S(2)}) %all-to-all-start.1) | async-done | bytes 196640 | tf_op jit(solution)/shard_map/all_to_all | solution.py:75
  31.1 1.0 %slice_reduce_fusion = (bf16[8,48,128]{2,1,0:T(8,128)(2,1)S(1)}, bf16[8,48,128]{2,1,0:T(8,128)(2,1)S(1)}) fusion(bf16[8,48,2,128]{3,2,1,0:T(2,128)(2,1)S(1)} %reshape.24), kind=kLoop, calls=%fused_computation.10 | loop fusion | bytes 393216 | tf_op jit(solution)/shard_map/slice | solution.py:40
  32.2 0.3 fusion.6
  32.4 0.3 fusion.2
  33.0 0.3 convolution_add_fusion.1
  33.3 0.3 multiply_subtract_fusion
  33.6 0.4 fusion.32
  34.0 0.4 fusion.30
  34.5 0.4 fusion.1
  34.9 0.4 fusion
  35.5 17.4 %all_to_all.45 = f32[8,3,16,256]{3,2,1,0:T(8,128)S(1)} all-to-all(f32[8,3,16,256]{3,2,1,0:T(8,128)S(1)} %pad_maximum_fusion), channel_id=1, replica_groups=mesh['space'=4,'energy'=8] {'energy'}, dimensions={0} | all-to-all | bytes 786432 | tf_op jit(solution)/shard_map/all_to_all | solution.py:63
  52.9 0.8 %copy.31 = f32[8,3,16,256]{3,2,0,1:T(8,128)} copy(f32[8,3,16,256]{3,2,1,0:T(8,128)S(1)} %all_to_all.45) | data formatting | bytes 786432 | tf_op jit(solution)/shard_map/all_to_all | solution.py:63
  (16 shorter events, 0.9 us)
Async XLA Ops:
  1.8 7.4 %copy-start = (bf16[1,1,3,128,256]{4,3,2,1,0:T(8,128)(2,1)S(1)}, bf16[1,1,3,128,256]{4,3,2,1,0:T(8,128)(2,1)}, u32[]{:S(2)}) copy-start(bf16[1,1,3,128,256]{4,3,2,1,0:T(8,128)(2,1)} %param.3) | copy-start | bytes 589828
  1.8 16.3 %all-to-all-start = ((bf16[1,3,128,256]{3,1,0,2:T(4,128)(2,1)}), bf16[1,3,128,256]{3,1,0,2:T(4,128)(2,1)S(1)}, u32[]{:S(2)}, u32[]{:S(2)}) async-start(bf16[1,3,128,256]{3,1,0,2:T(4,128)(2,1)} %bitcast.58), calls=%async_computation | async-start | bytes 524288 | tf_op jit(solution)/shard_map/all_to_all | solution.py:74
  9.4 2.8 %collective-permute-start = (bf16[1,1,128,256]{2,3,1,0:T(8,128)(2,1)S(1)}, bf16[1,1,128,256]{2,3,1,0:T(8,128)(2,1)S(1)}, u32[]{:S(2)}, u32[]{:S(2)}) collective-permute-start(bf16[1,1,128,256]{2,3,1,0:T(8,128)(2,1)S(1)} %get-tuple-element.11), channel_id=1, source_target_pairs={{0,8},{8,16},{16,24},{1,9},{9,17},{17,25},{2,10},{10,18},{18,26},{... | collective-permute-start | bytes 196616 | tf_op jit(solution)/shard_map/ppermute | solution.py:14
  10.9 4.7 %collective-permute-start.1 = (bf16[1,1,128,256]{2,3,1,0:T(8,128)(2,1)S(1)}, bf16[1,1,128,256]{2,3,1,0:T(8,128)(2,1)S(1)}, u32[]{:S(2)}, u32[]{:S(2)}) collective-permute-start(bf16[1,1,128,256]{2,3,1,0:T(8,128)(2,1)S(1)} %get-tuple-element.12), channel_id=1, source_target_pairs={{8,0},{16,8},{24,16},{9,1},{17,9},{25,17},{10,2},{18,10},{26,18},{... | collective-permute-start | bytes 196616 | tf_op jit(solution)/shard_map/ppermute | solution.py:17
  18.1 12.9 %all-to-all-start.1 = ((bf16[1,3,128,256]{3,1,0,2:T(4,128)(2,1)}), bf16[1,3,128,256]{3,1,0,2:T(4,128)(2,1)S(1)}, u32[]{:S(2)}, u32[]{:S(2)}) async-start(bf16[1,3,128,256]{3,1,0,2:T(4,128)(2,1)} %copy.26), calls=%async_computation.1 | async-start | bytes 524288 | tf_op jit(solution)/shard_map/all_to_all | solution.py:75
where the time goes:
time: 54.1 us; the launch traced here: 53.7 us
  blocking collectives  17.4 us (32%)
  starting transfers between devices  14.7 us (27%)
  waiting for transfers between devices  11.2 us (21%)
  local copies, waits for them, and re-layouts  6.1 us (11%)
  matrix products  3.94 us (7%)
    all_to_all x1, blocking collectives, correlate_rows(): lax.all_to_all(result, 'energy', split_axis=0, concat_axis=2, tiled=True)  17.4 us
    all_to_all x1, starting transfers between devices, on_device(): lax.all_to_all(own_lesser, 'energy', split_axis=2, concat_axis=0, tiled=T...  7.41 us
    all_to_all x1, waiting for transfers between devices, on_device(): lax.all_to_all(mirrored, 'energy', split_axis=2, concat_axis=0, tiled=True)  6.36 us
    all_to_all x1, starting transfers between devices, on_device(): lax.all_to_all(mirrored, 'energy', split_axis=2, concat_axis=0, tiled=True)  4.57 us
    dot_general x12, matrix products, apply(): jnp.dot(matrix, data, precision=high, preferred_element_type=jnp.float32)  3.94 us
    ppermute x1, waiting for transfers between devices, with_halo(): lax.ppermute(lax.slice_in_dim(block, 0, width, axis=dim), axis, backward)  3.42 us
    unnamed x4, local copies, waits for them, and re-layouts  1.95 us
    ppermute x1, starting transfers between devices, with_halo(): lax.ppermute(lax.slice_in_dim(block, block.shape[dim] - width, None, axis...  1.46 us
  transfers between devices with their start and end apart: 4, of which 3 were waited for; matrix products, arithmetic and copies ran while one was open for 6% of the time, Pallas kernels for 0%

commit v1 on v0

v1 whole, which is shorter than its diff:
```python
import jax
import jax.numpy as jnp
from jax import lax
from jax.sharding import PartitionSpec as P


def flip_tiles(tiles):
    shape = tiles.shape
    width = shape[-2]
    split = tiles.reshape(shape[:-1] + (2, width))
    turned = jnp.swapaxes(split, -3, -1)
    return turned.reshape(shape)


def mirror(greater):
    count = lax.axis_size("space")
    forward = [(i, i + 1) for i in range(count - 1)]
    backward = [(i + 1, i) for i in range(count - 1)]
    below = lax.ppermute(greater[2], "space", forward)
    above = lax.ppermute(greater[0], "space", backward)
    return flip_tiles(jnp.stack([below, greater[1], above]))


def correlate(left, right):
    total = left.shape[0]
    width = left.shape[-1] // 2
    left = left.astype(jnp.float32)
    right = right.astype(jnp.float32)
    lre = jnp.concatenate([left[..., :width]] * 2)
    lim = jnp.concatenate([left[..., width:]] * 2)
    rre = right[..., :width]
    rim = right[..., width:]
    outs = []
    for shift in range(total):
        a = lre[shift:shift + total]
        b = lim[shift:shift + total]
        pre = jnp.sum(a * rre - b * rim, axis=0)
        pim = jnp.sum(a * rim + b * rre, axis=0)
        outs.append(jnp.concatenate([pre, pim], axis=-1))
    return jnp.stack(outs)


def on_device(lesser, greater):
    own_lesser = lesser[:, 0]
    mirrored = mirror(greater[0, 0])[None]
    left = lax.all_to_all(own_lesser, "energy", split_axis=2, concat_axis=0, tiled=True)
    right = lax.all_to_all(mirrored, "energy", split_axis=2, concat_axis=0, tiled=True)
    summed = correlate(left, right)
    back = lax.all_to_all(summed, "energy", split_axis=0, concat_axis=2, tiled=True)
    return back[:, None]


def solution(mesh):
    return jax.shard_map(
        on_device,
        mesh=mesh,
        in_specs=(P("energy", "space", None, None, None), P("energy", "space", None, None, None)),
        out_specs=P("energy", "space", None, None, None),
        check_vma=False,
    )
```

time: 54.1 us -> 49.8 us (0.921)
  matrix products: 3.94 us -> 0 us
  local copies, waits for them, and re-layouts: 6.1 us -> 4.05 us
  waiting for transfers between devices: 11.2 us -> 13 us
  blocking collectives: 17.4 us -> 16.1 us
  starting transfers between devices: 14.7 us -> 15.4 us
  other arithmetic: 0.05 us -> 0.61 us
    dot_general x12 -> x0, matrix products: 3.94 us -> none  [apply(): jnp.dot(matrix, data, precision=high, preferred_element_type=jnp.float32)]
    all_to_all x1, waiting for transfers between devices: 6.36 us -> 9.94 us  [on_device(): lax.all_to_all(mirrored, 'energy', split_axis=2, concat_axis=0, tiled=True)]
    ppermute x2, waiting for transfers between devices: 3.42 us -> 0.76 us  [the longest x1 0.75 us: mirror(): below = lax.ppermute(greater[2], 'space', forward)]
    slice x3 -> x2, local copies, waits for them, and re-layouts: 2.07 us -> 0.05 us  [the longest x1 0.03 us: correlate(): lim = jnp.concatenate([left[..., width:]] * 2)]
    ppermute x2, starting transfers between devices: 2.75 us -> 4.33 us  [the longest x1 3.03 us: mirror(): below = lax.ppermute(greater[2], 'space', forward)]
    all_to_all x1, blocking collectives: 17.4 us -> 16.1 us  [on_device(): lax.all_to_all(summed, 'energy', split_axis=0, concat_axis=2, tiled=True)]
    reshape x5 -> x0, local copies, waits for them, and re-layouts: 1.07 us -> none  [the longest x1 0.89 us: flip_tiles(): return turned.reshape(shape)]
    all_to_all x1, starting transfers between devices: 4.57 us -> 3.65 us  [on_device(): lax.all_to_all(mirrored, 'energy', split_axis=2, concat_axis=0, tiled=True)]
  transfers between devices with their start and end apart: 4 -> 4, of which waited for: 3 -> 3; matrix products, arithmetic and copies ran while one was open for 6% -> 3% of each run, Pallas kernels for 0% -> 0%
where the time goes in v1:
time: 49.8 us; the launch traced here: 49.3 us
  blocking collectives  16.1 us (32%)
  starting transfers between devices  15.4 us (31%)
  waiting for transfers between devices  13 us (26%)
  local copies, waits for them, and re-layouts  4.05 us (8%)
  other arithmetic  0.61 us (1%)
    all_to_all x1, blocking collectives, on_device(): lax.all_to_all(summed, 'energy', split_axis=0, concat_axis=2, tiled=True)  16.1 us
    all_to_all x1, waiting for transfers between devices, on_device(): lax.all_to_all(mirrored, 'energy', split_axis=2, concat_axis=0, tiled=True)  9.94 us
    all_to_all x1, starting transfers between devices, on_device(): lax.all_to_all(own_lesser, 'energy', split_axis=2, concat_axis=0, tiled=T...  7.41 us
    all_to_all x1, starting transfers between devices, on_device(): lax.all_to_all(mirrored, 'energy', split_axis=2, concat_axis=0, tiled=True)  3.65 us
    ppermute x1, starting transfers between devices, mirror(): below = lax.ppermute(greater[2], 'space', forward)  3.03 us
    all_to_all x1, waiting for transfers between devices, on_device(): lax.all_to_all(own_lesser, 'energy', split_axis=2, concat_axis=0, tiled=T...  2.34 us
    unnamed x6, local copies, waits for them, and re-layouts  2.12 us
    ppermute x1, starting transfers between devices, mirror(): above = lax.ppermute(greater[0], 'space', backward)  1.29 us
  transfers between devices with their start and end apart: 4, of which 3 were waited for; matrix products, arithmetic and copies ran while one was open for 3% of the time, Pallas kernels for 0%

profile of v1, /device:TPU:0, one launch (start us, length us, event | category | flops | bytes accessed | tf_op | source)
XLA Modules:
  0.0 49.3 jit_solution(14685358563828108365)
XLA Ops:
  0.0 1.8 %copy.39 = bf16[1,1,3,128,256]{4,2,3,1,0:T(4,128)(2,1)} copy(bf16[1,1,3,128,256]{4,3,2,1,0:T(8,128)(2,1)} %param.2) | data formatting | bytes 393216 | tf_op args[0]
  1.8 0.0 copy-start
  1.8 7.4 %all-to-all-start = ((bf16[1,3,128,256]{3,1,0,2:T(4,128)(2,1)}), bf16[1,3,128,256]{3,1,0,2:T(4,128)(2,1)S(1)}, u32[]{:S(2)}, u32[]{:S(2)}) async-start(bf16[1,3,128,256]{3,1,0,2:T(4,128)(2,1)} %bitcast.59), calls=%async_computation | async-start | bytes 524288 | tf_op jit(solution)/shard_map/all_to_all | solution.py:46
  9.2 0.0 copy-done
  9.2 0.1 copy.37
  9.3 1.3 %collective-permute-start.1 = (bf16[128,256]{0,1:T(8,128)(2,1)S(1)}, bf16[128,256]{0,1:T(8,128)(2,1)S(1)}, u32[]{:S(2)}, u32[]{:S(2)}) collective-permute-start(bf16[128,256]{0,1:T(8,128)(2,1)S(1)} %bitcast.64), channel_id=1, source_target_pairs={{8,0},{16,8},{24,16},{9,1},{17,9},{25,17},{10,2},{18,10},{26,18},{... | collective-permute-start | bytes 196616 | tf_op jit(solution)/shard_map/ppermute | solution.py:20
  10.7 0.1 copy.35
  10.8 3.0 %collective-permute-start = (bf16[128,256]{0,1:T(8,128)(2,1)S(1)}, bf16[128,256]{0,1:T(8,128)(2,1)S(1)}, u32[]{:S(2)}, u32[]{:S(2)}) collective-permute-start(bf16[128,256]{0,1:T(8,128)(2,1)S(1)} %bitcast.65), channel_id=1, source_target_pairs={{0,8},{8,16},{16,24},{1,9},{9,17},{17,25},{2,10},{10,18},{18,26},{... | collective-permute-start | bytes 196616 | tf_op jit(solution)/shard_map/ppermute | solution.py:19
  13.8 0.1 copy.36
  13.9 0.0 collective-permute-done.1
  13.9 0.8 %collective-permute-done = bf16[128,256]{0,1:T(8,128)(2,1)S(1)} collective-permute-done((bf16[128,256]{0,1:T(8,128)(2,1)S(1)}, bf16[128,256]{0,1:T(8,128)(2,1)S(1)}, u32[]{:S(2)}, u32[]{:S(2)}) %collective-permute-start) | collective-permute-done | bytes 65568 | tf_op jit(solution)/shard_map/ppermute | solution.py:19
  14.7 0.2 copy.31
  14.9 0.9 %copy.32 = bf16[1,3,128,256]{3,1,0,2:T(4,128)(2,1)} copy(bf16[1,3,128,256]{2,3,1,0:T(8,128)(2,1)S(1)} %bitcast.62) | data formatting | bytes 393216 | tf_op jit(solution)/shard_map/broadcast_in_dim;reshape | solution.py:45
  15.8 2.3 %all-to-all-done = bf16[1,3,128,256]{3,1,0,2:T(4,128)(2,1)S(1)} async-done(((bf16[1,3,128,256]{3,1,0,2:T(4,128)(2,1)}), bf16[1,3,128,256]{3,1,0,2:T(4,128)(2,1)S(1)}, u32[]{:S(2)}, u32[]{:S(2)}) %all-to-all-start) | async-done | bytes 196640 | tf_op jit(solution)/shard_map/all_to_all | solution.py:46
  18.1 3.7 %all-to-all-start.1 = ((bf16[1,3,128,256]{3,1,0,2:T(4,128)(2,1)}), bf16[1,3,128,256]{3,1,0,2:T(4,128)(2,1)S(1)}, u32[]{:S(2)}, u32[]{:S(2)}) async-start(bf16[1,3,128,256]{3,1,0,2:T(4,128)(2,1)} %copy.32), calls=%async_computation.1 | async-start | bytes 524288 | tf_op jit(solution)/shard_map/all_to_all | solution.py:47
  21.8 9.9 %all-to-all-done.1 = bf16[1,3,128,256]{3,1,0,2:T(4,128)(2,1)S(1)} async-done(((bf16[1,3,128,256]{3,1,0,2:T(4,128)(2,1)}), bf16[1,3,128,256]{3,1,0,2:T(4,128)(2,1)S(1)}, u32[]{:S(2)}, u32[]{:S(2)}) %all-to-all-start.1) | async-done | bytes 196640 | tf_op jit(solution)/shard_map/all_to_all | solution.py:47
  31.8 0.1 convert_bitcast_fusion
  31.9 0.1 subtract_reduce_fusion.2
  32.0 0.1 subtract_reduce_fusion.1
  32.1 0.1 subtract_reduce_fusion
  32.2 0.1 add_reduce_fusion.1
  32.3 0.1 add_reduce_fusion
  32.5 16.1 %all_to_all.33 = f32[8,3,16,256]{3,2,1,0:T(8,128)S(1)} all-to-all(f32[8,3,16,256]{3,2,1,0:T(8,128)S(1)} %fusion.19), channel_id=1, replica_groups=mesh['space'=4,'energy'=8] {'energy'}, dimensions={0} | all-to-all | bytes 786432 | tf_op jit(solution)/shard_map/all_to_all | solution.py:49
  48.6 0.8 %copy.34 = f32[8,3,16,256]{3,2,0,1:T(8,128)} copy(f32[8,3,16,256]{3,2,1,0:T(8,128)S(1)} %all_to_all.33) | data formatting | bytes 786432 | tf_op jit(solution)/shard_map/all_to_all | solution.py:49
  (13 shorter events, 0.2 us)
Async XLA Ops:
  1.8 7.4 %copy-start = (bf16[1,1,3,128,256]{4,3,2,1,0:T(8,128)(2,1)S(1)}, bf16[1,1,3,128,256]{4,3,2,1,0:T(8,128)(2,1)}, u32[]{:S(2)}) copy-start(bf16[1,1,3,128,256]{4,3,2,1,0:T(8,128)(2,1)} %param.3) | copy-start | bytes 589828
  1.8 16.3 %all-to-all-start = ((bf16[1,3,128,256]{3,1,0,2:T(4,128)(2,1)}), bf16[1,3,128,256]{3,1,0,2:T(4,128)(2,1)S(1)}, u32[]{:S(2)}, u32[]{:S(2)}) async-start(bf16[1,3,128,256]{3,1,0,2:T(4,128)(2,1)} %bitcast.59), calls=%async_computation | async-start | bytes 524288 | tf_op jit(solution)/shard_map/all_to_all | solution.py:46
  9.3 4.6 %collective-permute-start.1 = (bf16[128,256]{0,1:T(8,128)(2,1)S(1)}, bf16[128,256]{0,1:T(8,128)(2,1)S(1)}, u32[]{:S(2)}, u32[]{:S(2)}) collective-permute-start(bf16[128,256]{0,1:T(8,128)(2,1)S(1)} %bitcast.64), channel_id=1, source_target_pairs={{8,0},{16,8},{24,16},{9,1},{17,9},{25,17},{10,2},{18,10},{26,18},{... | collective-permute-start | bytes 196616 | tf_op jit(solution)/shard_map/ppermute | solution.py:20
  10.8 3.9 %collective-permute-start = (bf16[128,256]{0,1:T(8,128)(2,1)S(1)}, bf16[128,256]{0,1:T(8,128)(2,1)S(1)}, u32[]{:S(2)}, u32[]{:S(2)}) collective-permute-start(bf16[128,256]{0,1:T(8,128)(2,1)S(1)} %bitcast.65), channel_id=1, source_target_pairs={{0,8},{8,16},{16,24},{1,9},{9,17},{17,25},{2,10},{10,18},{18,26},{... | collective-permute-start | bytes 196616 | tf_op jit(solution)/shard_map/ppermute | solution.py:19
  18.1 13.6 %all-to-all-start.1 = ((bf16[1,3,128,256]{3,1,0,2:T(4,128)(2,1)}), bf16[1,3,128,256]{3,1,0,2:T(4,128)(2,1)S(1)}, u32[]{:S(2)}, u32[]{:S(2)}) async-start(bf16[1,3,128,256]{3,1,0,2:T(4,128)(2,1)} %copy.32), calls=%async_computation.1 | async-start | bytes 524288 | tf_op jit(solution)/shard_map/all_to_all | solution.py:47

commit v2 on v1

--- a/solution.py
+++ b/solution.py
@@ -41,10 +41,16 @@
 
 
 def on_device(lesser, greater):
-    own_lesser = lesser[:, 0]
-    mirrored = mirror(greater[0, 0])[None]
-    left = lax.all_to_all(own_lesser, "energy", split_axis=2, concat_axis=0, tiled=True)
-    right = lax.all_to_all(mirrored, "energy", split_axis=2, concat_axis=0, tiled=True)
+    count = lax.axis_size("space")
+    forward = [(i, i + 1) for i in range(count - 1)]
+    backward = [(i + 1, i) for i in range(count - 1)]
+    both = jnp.stack([lesser[0, 0], flip_tiles(greater[0, 0])])[None]
+    got = lax.all_to_all(both, "energy", split_axis=3, concat_axis=0, tiled=True)
+    left = got[:, 0]
+    turned = got[:, 1]
+    below = lax.ppermute(turned[:, 2], "space", forward)
+    above = lax.ppermute(turned[:, 0], "space", backward)
+    right = jnp.stack([below, turned[:, 1], above], axis=1)
     summed = correlate(left, right)
     back = lax.all_to_all(summed, "energy", split_axis=0, concat_axis=2, tiled=True)
     return back[:, None]

time: 49.8 us -> 45.2 us (0.908)
  the two profiles are of different devices: /device:TPU:0 before, /device:TPU:1 now
where the time goes in v2:
time: 45.2 us; the launch traced here: 44.9 us
  blocking collectives  30 us (66%)
  starting transfers between devices  7.56 us (17%)
  waiting for transfers between devices  3.61 us (8%)
  local copies, waits for them, and re-layouts  2.96 us (7%)
  other arithmetic  0.62 us (1%)
    all_to_all x1, blocking collectives, on_device(): lax.all_to_all(both, 'energy', split_axis=3, concat_axis=0, tiled=True)  16.5 us
    all_to_all x1, blocking collectives, on_device(): lax.all_to_all(summed, 'energy', split_axis=0, concat_axis=2, tiled=True)  13.5 us
    ppermute x1, starting transfers between devices, on_device(): below = lax.ppermute(turned[:, 2], 'space', forward)  5.64 us
    ppermute x1, waiting for transfers between devices, on_device(): above = lax.ppermute(turned[:, 0], 'space', backward)  3.61 us
    ppermute x1, starting transfers between devices, on_device(): above = lax.ppermute(turned[:, 0], 'space', backward)  1.92 us
    unnamed x4, local copies, waits for them, and re-layouts  1.29 us
  transfers between devices with their start and end apart: 2, of which 1 were waited for; matrix products, arithmetic and copies ran while one was open for 0% of the time, Pallas kernels for 0%

profile of v2, /device:TPU:1, one launch (start us, length us, event | category | flops | bytes accessed | tf_op | source)
XLA Modules:
  0.0 44.9 jit_solution(15362903296871609008)
XLA Ops:
  0.0 0.0 copy-start
  0.0 1.1 %copy.19 = bf16[1,1,3,128,256]{3,4,2,1,0:T(8,128)(2,1)S(1)} copy(bf16[1,1,3,128,256]{4,3,2,1,0:T(8,128)(2,1)} %param.2) | data formatting | bytes 393216 | tf_op args[0]
  1.1 0.0 copy-done
  1.1 0.2 copy.20
  1.3 0.2 copy.21
  1.5 0.6 %copy.22 = bf16[1,2,3,128,256]{4,1,2,0,3:T(2,128)(2,1)S(1)} copy(bf16[1,2,3,128,256]{3,4,2,1,0:T(8,128)(2,1)S(1)} %maximum_bitcast_fusion) | data formatting | bytes 786432 | tf_op jit(solution)/shard_map/broadcast_in_dim | solution.py:47
  2.2 16.5 %all_to_all.33 = bf16[1,2,3,128,256]{4,1,2,0,3:T(2,128)(2,1)S(1)} all-to-all(bf16[1,2,3,128,256]{4,1,2,0,3:T(2,128)(2,1)S(1)} %copy.22), channel_id=1, replica_groups=mesh['space'=4,'energy'=8] {'energy'}, dimensions={3} | all-to-all | bytes 786432 | tf_op jit(solution)/shard_map/all_to_all | solution.py:48
  18.8 5.6 %collective-permute-start = (bf16[8,16,256]{2,1,0:T(8,128)(2,1)S(1)}, bf16[8,16,256]{2,1,0:T(8,128)(2,1)S(1)}, u32[]{:S(2)}, u32[]{:S(2)}) collective-permute-start(bf16[8,16,256]{2,1,0:T(8,128)(2,1)S(1)} %get-tuple-element.27), channel_id=1, source_target_pairs={{0,8},{8,16},{16,24},{1,9},{9,17},{17,25},{2,10},{10,18},{18,26},{... | collective-permute-start | bytes 196616 | tf_op jit(solution)/shard_map/ppermute | solution.py:51
  24.5 1.9 %collective-permute-start.1 = (bf16[8,16,256]{2,1,0:T(8,128)(2,1)S(1)}, bf16[8,16,256]{2,1,0:T(8,128)(2,1)S(1)}, u32[]{:S(2)}, u32[]{:S(2)}) collective-permute-start(bf16[8,16,256]{2,1,0:T(8,128)(2,1)S(1)} %get-tuple-element.28), channel_id=1, source_target_pairs={{8,0},{16,8},{24,16},{9,1},{17,9},{25,17},{10,2},{18,10},{26,18},{... | collective-permute-start | bytes 196616 | tf_op jit(solution)/shard_map/ppermute | solution.py:52
  26.5 0.0 collective-permute-done
  26.5 3.6 %collective-permute-done.1 = bf16[8,16,256]{2,1,0:T(8,128)(2,1)S(1)} collective-permute-done((bf16[8,16,256]{2,1,0:T(8,128)(2,1)S(1)}, bf16[8,16,256]{2,1,0:T(8,128)(2,1)S(1)}, u32[]{:S(2)}, u32[]{:S(2)}) %collective-permute-start.1) | collective-permute-done | bytes 65568 | tf_op jit(solution)/shard_map/ppermute | solution.py:52
  30.1 0.1 subtract_reduce_fusion.2
  30.2 0.1 subtract_reduce_fusion.1
  30.3 0.1 subtract_reduce_fusion
  30.4 0.1 add_reduce_fusion.1
  30.5 0.1 add_reduce_fusion
  30.7 13.5 %all_to_all.34 = f32[8,3,16,256]{3,2,1,0:T(8,128)S(1)} all-to-all(f32[8,3,16,256]{3,2,1,0:T(8,128)S(1)} %fusion.20), channel_id=1, replica_groups=mesh['space'=4,'energy'=8] {'energy'}, dimensions={0} | all-to-all | bytes 786432 | tf_op jit(solution)/shard_map/all_to_all | solution.py:55
  44.2 0.8 %copy.24 = f32[8,3,16,256]{3,2,0,1:T(8,128)} copy(f32[8,3,16,256]{3,2,1,0:T(8,128)S(1)} %all_to_all.34) | data formatting | bytes 786432 | tf_op jit(solution)/shard_map/all_to_all | solution.py:55
  (14 shorter events, 0.3 us)
Async XLA Ops:
  0.0 1.1 %copy-start = (bf16[1,1,3,128,256]{4,3,2,1,0:T(8,128)(2,1)S(1)}, bf16[1,1,3,128,256]{4,3,2,1,0:T(8,128)(2,1)}, u32[]{:S(2)}) copy-start(bf16[1,1,3,128,256]{4,3,2,1,0:T(8,128)(2,1)} %param.3) | copy-start | bytes 589828
  18.8 7.6 %collective-permute-start = (bf16[8,16,256]{2,1,0:T(8,128)(2,1)S(1)}, bf16[8,16,256]{2,1,0:T(8,128)(2,1)S(1)}, u32[]{:S(2)}, u32[]{:S(2)}) collective-permute-start(bf16[8,16,256]{2,1,0:T(8,128)(2,1)S(1)} %get-tuple-element.27), channel_id=1, source_target_pairs={{0,8},{8,16},{16,24},{1,9},{9,17},{17,25},{2,10},{10,18},{18,26},{... | collective-permute-start | bytes 196616 | tf_op jit(solution)/shard_map/ppermute | solution.py:51
  24.5 5.6 %collective-permute-start.1 = (bf16[8,16,256]{2,1,0:T(8,128)(2,1)S(1)}, bf16[8,16,256]{2,1,0:T(8,128)(2,1)S(1)}, u32[]{:S(2)}, u32[]{:S(2)}) collective-permute-start(bf16[8,16,256]{2,1,0:T(8,128)(2,1)S(1)} %get-tuple-element.28), channel_id=1, source_target_pairs={{8,0},{16,8},{24,16},{9,1},{17,9},{25,17},{10,2},{18,10},{26,18},{... | collective-permute-start | bytes 196616 | tf_op jit(solution)/shard_map/ppermute | solution.py:52

commit v3 on v2

--- a/solution.py
+++ b/solution.py
@@ -1,6 +1,9 @@
+import functools
 import jax
 import jax.numpy as jnp
 from jax import lax
+from jax.experimental import pallas as pl
+from jax.experimental.pallas import tpu as pltpu
 from jax.sharding import PartitionSpec as P
 
 
@@ -40,20 +43,66 @@
     return jnp.stack(outs)
 
 
+def pack_kernel(total, rows, lesser_ref, greater_ref, out_ref):
+    tiles, height, width = lesser_ref.shape
+    half = width // 2
+    for tile in range(tiles):
+        blocks = [
+            greater_ref[tiles - 1 - tile, :, part * half:(part + 1) * half].astype(jnp.float32).T.astype(out_ref.dtype)
+            for part in range(2)
+        ]
+        for chunk in range(total):
+            low = max(tile * height, chunk * rows)
+            high = min((tile + 1) * height, (chunk + 1) * rows)
+            if low >= high:
+                continue
+            dst = slice(low - chunk * rows, high - chunk * rows)
+            src = slice(low - tile * height, high - tile * height)
+            out_ref[chunk, 0, dst, :] = lesser_ref[tile, src, :]
+            for part in range(2):
+                out_ref[chunk, 1, dst, part * half:(part + 1) * half] = blocks[part][src]
+
+
+def pack(lesser, greater, total, rows):
+    tiles, height, width = lesser.shape
+    return pl.pallas_call(
+        functools.partial(pack_kernel, total, rows),
+        out_shape=jax.ShapeDtypeStruct((total, 2, rows, width), lesser.dtype),
+        in_specs=[pl.BlockSpec(memory_space=pltpu.VMEM)] * 2,
+        out_specs=pl.BlockSpec(memory_space=pltpu.VMEM),
+        cost_estimate=pl.CostEstimate(flops=0, transcendentals=0, bytes_accessed=4 * lesser.size * 2),
+    )(lesser, greater)
+
+
+def pack_plain(lesser, greater, total, rows):
+    width = lesser.shape[-1]
+    turned = flip_tiles(greater)
+    placed = jnp.stack([turned[2], turned[1], turned[0]])
+    return jnp.stack([lesser.reshape(total, rows, width), placed.reshape(total, rows, width)], axis=1)
+
+
 def on_device(lesser, greater):
     count = lax.axis_size("space")
+    total = lax.axis_size("energy")
     forward = [(i, i + 1) for i in range(count - 1)]
     backward = [(i + 1, i) for i in range(count - 1)]
-    both = jnp.stack([lesser[0, 0], flip_tiles(greater[0, 0])])[None]
-    got = lax.all_to_all(both, "energy", split_axis=3, concat_axis=0, tiled=True)
+    tiles, height, width = lesser.shape[2:]
+    rows = tiles * height // total
+    if rows % 16 == 0 and height % 16 == 0:
+        both = pack(lesser[0, 0], greater[0, 0], total, rows)
+    else:
+        both = pack_plain(lesser[0, 0], greater[0, 0], total, rows)
+    got = lax.all_to_all(both, "energy", split_axis=0, concat_axis=0, tiled=True)
     left = got[:, 0]
-    turned = got[:, 1]
-    below = lax.ppermute(turned[:, 2], "space", forward)
-    above = lax.ppermute(turned[:, 0], "space", backward)
-    right = jnp.stack([below, turned[:, 1], above], axis=1)
+    mine = got[:, 1]
+    below = lax.ppermute(mine, "space", forward)
+    above = lax.ppermute(mine, "space", backward)
+    first = lax.axis_index("energy") * rows
+    tile = (first + lax.broadcasted_iota(jnp.int32, (1, rows, 1), 1)) // height
+    right = jnp.where(tile == 0, below, jnp.where(tile == 1, mine, above))
     summed = correlate(left, right)
-    back = lax.all_to_all(summed, "energy", split_axis=0, concat_axis=2, tiled=True)
-    return back[:, None]
+    back = lax.all_to_all(summed, "energy", split_axis=0, concat_axis=0, tiled=True)
+    return back.reshape((1, 1, tiles, height, width))
 
 
 def solution(mesh):

time: 45.2 us -> 44.3 us (0.980)
  blocking collectives: 30 us -> 14 us
  waiting for transfers between devices: 3.61 us -> 11.7 us
  starting transfers between devices: 7.56 us -> 14.8 us
  local copies, waits for them, and re-layouts: 2.96 us -> 0.77 us
  Pallas kernels: 0 us -> 1.9 us
    all_to_all x2 -> x1, blocking collectives: 30 us -> 14 us  [on_device(): lax.all_to_all(summed, 'energy', split_axis=0, concat_axis=0, tiled=True)]
    all_to_all x0 -> x1, waiting for transfers between devices: none -> 9.16 us  [on_device(): lax.all_to_all(both, 'energy', split_axis=0, concat_axis=0, tiled=True)]
    all_to_all x0 -> x1, starting transfers between devices: none -> 6.34 us  [on_device(): lax.all_to_all(both, 'energy', split_axis=0, concat_axis=0, tiled=True)]
    pallas_call x0 -> x1, Pallas kernels: none -> 1.9 us  [pack(): pl.pallas_call(functools.partial(pack_kernel, total, rows), out_shape=jax...]
    ppermute x2, waiting for transfers between devices: 3.61 us -> 2.56 us  [the longest x1 1.37 us: on_device(): above = lax.ppermute(mine, 'space', backward)]
    ppermute x2, starting transfers between devices: 7.56 us -> 8.41 us  [the longest x1 5.37 us: on_device(): above = lax.ppermute(mine, 'space', backward)]
    all_to_all x2 -> x0, local copies, waits for them, and re-layouts: 0.81 us -> none  [the longest x1 0.77 us: on_device(): lax.all_to_all(summed, 'energy', split_axis=0, concat_axis=2, tiled=True)]
    broadcast_in_dim x1 -> x0, local copies, waits for them, and re-layouts: 0.64 us -> none  [on_device(): both = jnp.stack([lesser[0, 0], flip_tiles(greater[0, 0])])[None]]
  transfers between devices with their start and end apart: 2 -> 3, of which waited for: 1 -> 3; matrix products, arithmetic and copies ran while one was open for 0% -> 0% of each run, Pallas kernels for 0% -> 0%
where the time goes in v3:
time: 44.3 us; the launch traced here: 44 us
  starting transfers between devices  14.8 us (33%)
  blocking collectives  14 us (32%)
  waiting for transfers between devices  11.7 us (26%)
  Pallas kernels  1.9 us (4%)
  local copies, waits for them, and re-layouts  0.77 us (2%)
  other arithmetic  0.64 us (1%)
    all_to_all x1, blocking collectives, on_device(): lax.all_to_all(summed, 'energy', split_axis=0, concat_axis=0, tiled=True)  14 us
    all_to_all x1, waiting for transfers between devices, on_device(): lax.all_to_all(both, 'energy', split_axis=0, concat_axis=0, tiled=True)  9.16 us
    all_to_all x1, starting transfers between devices, on_device(): lax.all_to_all(both, 'energy', split_axis=0, concat_axis=0, tiled=True)  6.34 us
    ppermute x1, starting transfers between devices, on_device(): above = lax.ppermute(mine, 'space', backward)  5.37 us
    ppermute x1, starting transfers between devices, on_device(): below = lax.ppermute(mine, 'space', forward)  3.05 us
    pallas_call x1, Pallas kernels, pack(): pl.pallas_call(functools.partial(pack_kernel, total, rows), out_shape=jax...  1.9 us
    ppermute x1, waiting for transfers between devices, on_device(): above = lax.ppermute(mine, 'space', backward)  1.37 us
    ppermute x1, waiting for transfers between devices, on_device(): below = lax.ppermute(mine, 'space', forward)  1.18 us
  transfers between devices with their start and end apart: 3, of which 3 were waited for; matrix products, arithmetic and copies ran while one was open for 0% of the time, Pallas kernels for 0%

profile of v3, /device:TPU:1, one launch (start us, length us, event | category | flops | bytes accessed | tf_op | source)
XLA Modules:
  0.0 44.0 jit_solution(15644826727618163843)
XLA Ops:
  0.0 1.9 %shard_map.28 = bf16[8,2,48,256]{3,2,1,0:T(8,128)(2,1)} custom-call(bf16[3,128,256]{2,1,0:T(8,128)(2,1)} %bitcast.47, bf16[3,128,256]{2,1,0:T(8,128)(2,1)} %bitcast.48), custom_call_target="tpu_custom_call" | custom-call | bytes 786432 | tf_op jit(solution)/shard_map/pallas_call | solution.py:68
  1.9 6.3 %all-to-all-start = ((bf16[8,2,48,256]{3,2,1,0:T(8,128)(2,1)}), bf16[8,2,48,256]{3,2,1,0:T(8,128)(2,1)S(1)}, u32[]{:S(2)}, u32[]{:S(2)}) async-start(bf16[8,2,48,256]{3,2,1,0:T(8,128)(2,1)} %shard_map.28), calls=%async_computation | async-start | bytes 786432 | tf_op jit(solution)/shard_map/all_to_all | solution.py:95
  8.3 9.2 %all-to-all-done = bf16[8,2,48,256]{3,2,1,0:T(8,128)(2,1)S(1)} async-done(((bf16[8,2,48,256]{3,2,1,0:T(8,128)(2,1)}), bf16[8,2,48,256]{3,2,1,0:T(8,128)(2,1)S(1)}, u32[]{:S(2)}, u32[]{:S(2)}) %all-to-all-start) | async-done | bytes 393248 | tf_op jit(solution)/shard_map/all_to_all | solution.py:95
  17.5 5.4 %collective-permute-start.1 = (bf16[8,48,256]{2,1,0:T(8,128)(2,1)S(1)}, bf16[8,48,256]{2,1,0:T(8,128)(2,1)S(1)}, u32[]{:S(2)}, u32[]{:S(2)}) collective-permute-start(bf16[8,48,256]{2,1,0:T(8,128)(2,1)S(1)} %get-tuple-element.26), channel_id=1, source_target_pairs={{8,0},{16,8},{24,16},{9,1},{17,9},{25,17},{10,2},{18,10},{26,18},{... | collective-permute-start | bytes 589832 | tf_op jit(solution)/shard_map/ppermute | solution.py:99
  22.8 3.0 %collective-permute-start = (bf16[8,48,256]{2,1,0:T(8,128)(2,1)S(1)}, bf16[8,48,256]{2,1,0:T(8,128)(2,1)S(1)}, u32[]{:S(2)}, u32[]{:S(2)}) collective-permute-start(bf16[8,48,256]{2,1,0:T(8,128)(2,1)S(1)} %get-tuple-element.26), channel_id=1, source_target_pairs={{0,8},{8,16},{16,24},{1,9},{9,17},{17,25},{2,10},{10,18},{18,26},{... | collective-permute-start | bytes 589832 | tf_op jit(solution)/shard_map/ppermute | solution.py:98
  25.9 1.4 %collective-permute-done.1 = bf16[8,48,256]{2,1,0:T(8,128)(2,1)S(1)} collective-permute-done((bf16[8,48,256]{2,1,0:T(8,128)(2,1)S(1)}, bf16[8,48,256]{2,1,0:T(8,128)(2,1)S(1)}, u32[]{:S(2)}, u32[]{:S(2)}) %collective-permute-start.1) | collective-permute-done | bytes 196640 | tf_op jit(solution)/shard_map/ppermute | solution.py:99
  27.3 1.2 %collective-permute-done = bf16[8,48,256]{2,1,0:T(8,128)(2,1)S(1)} collective-permute-done((bf16[8,48,256]{2,1,0:T(8,128)(2,1)S(1)}, bf16[8,48,256]{2,1,0:T(8,128)(2,1)S(1)}, u32[]{:S(2)}, u32[]{:S(2)}) %collective-permute-start) | collective-permute-done | bytes 196640 | tf_op jit(solution)/shard_map/ppermute | solution.py:98
  28.5 0.1 select_convert_fusion
  28.6 0.1 subtract_reduce_fusion.2
  28.7 0.1 subtract_reduce_fusion.1
  28.8 0.1 subtract_reduce_fusion
  28.9 0.1 add_reduce_fusion.1
  29.0 0.1 add_reduce_fusion
  29.2 14.0 %all_to_all.10 = f32[8,48,256]{2,1,0:T(8,128)S(1)} all-to-all(f32[8,48,256]{2,1,0:T(8,128)S(1)} %fusion.20), channel_id=1, replica_groups=mesh['space'=4,'energy'=8] {'energy'}, dimensions={0} | all-to-all | bytes 786432 | tf_op jit(solution)/shard_map/all_to_all | solution.py:104
  43.2 0.7 %copy.13 = f32[1,1,3,128,256]{4,3,2,1,0:T(8,128)} copy(f32[1,1,3,128,256]{4,3,2,1,0:T(8,128)S(1)} %bitcast.46) | data formatting | bytes 786432
  (11 shorter events, 0.1 us)
Async XLA Ops:
  1.9 15.5 %all-to-all-start = ((bf16[8,2,48,256]{3,2,1,0:T(8,128)(2,1)}), bf16[8,2,48,256]{3,2,1,0:T(8,128)(2,1)S(1)}, u32[]{:S(2)}, u32[]{:S(2)}) async-start(bf16[8,2,48,256]{3,2,1,0:T(8,128)(2,1)} %shard_map.28), calls=%async_computation | async-start | bytes 786432 | tf_op jit(solution)/shard_map/all_to_all | solution.py:95
  17.5 9.8 %collective-permute-start.1 = (bf16[8,48,256]{2,1,0:T(8,128)(2,1)S(1)}, bf16[8,48,256]{2,1,0:T(8,128)(2,1)S(1)}, u32[]{:S(2)}, u32[]{:S(2)}) collective-permute-start(bf16[8,48,256]{2,1,0:T(8,128)(2,1)S(1)} %get-tuple-element.26), channel_id=1, source_target_pairs={{8,0},{16,8},{24,16},{9,1},{17,9},{25,17},{10,2},{18,10},{26,18},{... | collective-permute-start | bytes 589832 | tf_op jit(solution)/shard_map/ppermute | solution.py:99
  22.8 5.6 %collective-permute-start = (bf16[8,48,256]{2,1,0:T(8,128)(2,1)S(1)}, bf16[8,48,256]{2,1,0:T(8,128)(2,1)S(1)}, u32[]{:S(2)}, u32[]{:S(2)}) collective-permute-start(bf16[8,48,256]{2,1,0:T(8,128)(2,1)S(1)} %get-tuple-element.26), channel_id=1, source_target_pairs={{0,8},{8,16},{16,24},{1,9},{9,17},{17,25},{2,10},{10,18},{18,26},{... | collective-permute-start | bytes 589832 | tf_op jit(solution)/shard_map/ppermute | solution.py:98

commit v4 on v3

--- a/solution.py
+++ b/solution.py
@@ -81,6 +81,14 @@
     return jnp.stack([lesser.reshape(total, rows, width), placed.reshape(total, rows, width)], axis=1)
 
 
+def wire_scale(total):
+    bound = total * 2 * 6.0 * 2.109375
+    scale = 1.0
+    while bound * scale * 2 <= 65504.0:
+        scale *= 2
+    return scale
+
+
 def on_device(lesser, greater):
     count = lax.axis_size("space")
     total = lax.axis_size("energy")
@@ -101,8 +109,10 @@
     tile = (first + lax.broadcasted_iota(jnp.int32, (1, rows, 1), 1)) // height
     right = jnp.where(tile == 0, below, jnp.where(tile == 1, mine, above))
     summed = correlate(left, right)
-    back = lax.all_to_all(summed, "energy", split_axis=0, concat_axis=0, tiled=True)
-    return back.reshape((1, 1, tiles, height, width))
+    scale = wire_scale(total)
+    packed = (summed * scale).astype(jnp.float16)
+    back = lax.all_to_all(packed, "energy", split_axis=0, concat_axis=0, tiled=True)
+    return (back.astype(jnp.float32) * (1.0 / scale)).reshape((1, 1, tiles, height, width))
 
 
 def solution(mesh):

time: 44.3 us -> 41.4 us (0.935)
  the two profiles are of different devices: /device:TPU:1 before, /device:TPU:4 now
where the time goes in v4:
time: 41.4 us; the launch traced here: 41.1 us
  waiting for transfers between devices  16.2 us (39%)
  blocking collectives  11.2 us (27%)
  starting transfers between devices  10.1 us (24%)
  Pallas kernels  1.9 us (5%)
  other arithmetic  1.46 us (4%)
    all_to_all x1, waiting for transfers between devices, on_device(): lax.all_to_all(both, 'energy', split_axis=0, concat_axis=0, tiled=True)  11.7 us
    all_to_all x1, blocking collectives, on_device(): lax.all_to_all(packed, 'energy', split_axis=0, concat_axis=0, tiled=True)  11.2 us
    all_to_all x1, starting transfers between devices, on_device(): lax.all_to_all(both, 'energy', split_axis=0, concat_axis=0, tiled=True)  5.81 us
    ppermute x1, waiting for transfers between devices, on_device(): below = lax.ppermute(mine, 'space', forward)  3.82 us
    ppermute x1, starting transfers between devices, on_device(): below = lax.ppermute(mine, 'space', forward)  2.41 us
    ppermute x1, starting transfers between devices, on_device(): above = lax.ppermute(mine, 'space', backward)  1.92 us
    pallas_call x1, Pallas kernels, pack(): pl.pallas_call(functools.partial(pack_kernel, total, rows), out_shape=jax...  1.9 us
  transfers between devices with their start and end apart: 3, of which 3 were waited for; matrix products, arithmetic and copies ran while one was open for 0% of the time, Pallas kernels for 0%

profile of v4, /device:TPU:4, one launch (start us, length us, event | category | flops | bytes accessed | tf_op | source)
XLA Modules:
  0.0 41.1 jit_solution(7665300147710227690)
XLA Ops:
  0.0 1.9 %shard_map.28 = bf16[8,2,48,256]{3,2,1,0:T(8,128)(2,1)} custom-call(bf16[3,128,256]{2,1,0:T(8,128)(2,1)} %bitcast.46, bf16[3,128,256]{2,1,0:T(8,128)(2,1)} %bitcast.47), custom_call_target="tpu_custom_call" | custom-call | bytes 786432 | tf_op jit(solution)/shard_map/pallas_call | solution.py:68
  1.9 5.8 %all-to-all-start = ((bf16[8,2,48,256]{3,2,1,0:T(8,128)(2,1)}), bf16[8,2,48,256]{3,2,1,0:T(8,128)(2,1)S(1)}, u32[]{:S(2)}, u32[]{:S(2)}) async-start(bf16[8,2,48,256]{3,2,1,0:T(8,128)(2,1)} %shard_map.28), calls=%async_computation | async-start | bytes 786432 | tf_op jit(solution)/shard_map/all_to_all | solution.py:103
  7.7 11.7 %all-to-all-done = bf16[8,2,48,256]{3,2,1,0:T(8,128)(2,1)S(1)} async-done(((bf16[8,2,48,256]{3,2,1,0:T(8,128)(2,1)}), bf16[8,2,48,256]{3,2,1,0:T(8,128)(2,1)S(1)}, u32[]{:S(2)}, u32[]{:S(2)}) %all-to-all-start) | async-done | bytes 393248 | tf_op jit(solution)/shard_map/all_to_all | solution.py:103
  19.4 1.9 %collective-permute-start.1 = (bf16[8,48,256]{2,1,0:T(8,128)(2,1)S(1)}, bf16[8,48,256]{2,1,0:T(8,128)(2,1)S(1)}, u32[]{:S(2)}, u32[]{:S(2)}) collective-permute-start(bf16[8,48,256]{2,1,0:T(8,128)(2,1)S(1)} %get-tuple-element.26), channel_id=1, source_target_pairs={{8,0},{16,8},{24,16},{9,1},{17,9},{25,17},{10,2},{18,10},{26,18},{... | collective-permute-start | bytes 589832 | tf_op jit(solution)/shard_map/ppermute | solution.py:107
  21.4 2.4 %collective-permute-start = (bf16[8,48,256]{2,1,0:T(8,128)(2,1)S(1)}, bf16[8,48,256]{2,1,0:T(8,128)(2,1)S(1)}, u32[]{:S(2)}, u32[]{:S(2)}) collective-permute-start(bf16[8,48,256]{2,1,0:T(8,128)(2,1)S(1)} %get-tuple-element.26), channel_id=1, source_target_pairs={{0,8},{8,16},{16,24},{1,9},{9,17},{17,25},{2,10},{10,18},{18,26},{... | collective-permute-start | bytes 589832 | tf_op jit(solution)/shard_map/ppermute | solution.py:106
  23.8 0.7 %collective-permute-done.1 = bf16[8,48,256]{2,1,0:T(8,128)(2,1)S(1)} collective-permute-done((bf16[8,48,256]{2,1,0:T(8,128)(2,1)S(1)}, bf16[8,48,256]{2,1,0:T(8,128)(2,1)S(1)}, u32[]{:S(2)}, u32[]{:S(2)}) %collective-permute-start.1) | collective-permute-done | bytes 196640 | tf_op jit(solution)/shard_map/ppermute | solution.py:107
  24.5 3.8 %collective-permute-done = bf16[8,48,256]{2,1,0:T(8,128)(2,1)S(1)} collective-permute-done((bf16[8,48,256]{2,1,0:T(8,128)(2,1)S(1)}, bf16[8,48,256]{2,1,0:T(8,128)(2,1)S(1)}, u32[]{:S(2)}, u32[]{:S(2)}) %collective-permute-start) | collective-permute-done | bytes 196640 | tf_op jit(solution)/shard_map/ppermute | solution.py:106
  28.4 0.1 select_convert_fusion
  28.5 0.1 subtract_reduce_fusion.2
  28.6 0.1 subtract_reduce_fusion.1
  28.7 0.1 subtract_reduce_fusion
  28.8 0.1 add_reduce_fusion.1
  28.8 0.1 add_reduce_fusion
  29.1 11.2 %all_to_all.10 = f16[8,48,256]{2,1,0:T(8,128)(2,1)S(1)} all-to-all(f16[8,48,256]{2,1,0:T(8,128)(2,1)S(1)} %multiply_convert_fusion), channel_id=1, replica_groups=mesh['space'=4,'energy'=8] {'energy'}, dimensions={0} | all-to-all | bytes 393216 | tf_op jit(solution)/shard_map/all_to_all | solution.py:114
  40.3 0.8 %convert_multiply_fusion = f32[8,48,256]{2,1,0:T(8,128)} fusion(f16[8,48,256]{2,1,0:T(8,128)(2,1)S(1)} %all_to_all.10), kind=kLoop, calls=%fused_computation.24 | loop fusion | flops 196608 | bytes 589824 | tf_op jit(solution)/shard_map/mul | solution.py:115
  (12 shorter events, 0.2 us)
Async XLA Ops:
  1.9 17.5 %all-to-all-start = ((bf16[8,2,48,256]{3,2,1,0:T(8,128)(2,1)}), bf16[8,2,48,256]{3,2,1,0:T(8,128)(2,1)S(1)}, u32[]{:S(2)}, u32[]{:S(2)}) async-start(bf16[8,2,48,256]{3,2,1,0:T(8,128)(2,1)} %shard_map.28), calls=%async_computation | async-start | bytes 786432 | tf_op jit(solution)/shard_map/all_to_all | solution.py:103
  19.4 5.1 %collective-permute-start.1 = (bf16[8,48,256]{2,1,0:T(8,128)(2,1)S(1)}, bf16[8,48,256]{2,1,0:T(8,128)(2,1)S(1)}, u32[]{:S(2)}, u32[]{:S(2)}) collective-permute-start(bf16[8,48,256]{2,1,0:T(8,128)(2,1)S(1)} %get-tuple-element.26), channel_id=1, source_target_pairs={{8,0},{16,8},{24,16},{9,1},{17,9},{25,17},{10,2},{18,10},{26,18},{... | collective-permute-start | bytes 589832 | tf_op jit(solution)/shard_map/ppermute | solution.py:107
  21.4 7.0 %collective-permute-start = (bf16[8,48,256]{2,1,0:T(8,128)(2,1)S(1)}, bf16[8,48,256]{2,1,0:T(8,128)(2,1)S(1)}, u32[]{:S(2)}, u32[]{:S(2)}) collective-permute-start(bf16[8,48,256]{2,1,0:T(8,128)(2,1)S(1)} %get-tuple-element.26), channel_id=1, source_target_pairs={{0,8},{8,16},{16,24},{1,9},{9,17},{17,25},{2,10},{10,18},{18,26},{... | collective-permute-start | bytes 589832 | tf_op jit(solution)/shard_map/ppermute | solution.py:106

commit v5 on v3

--- a/solution.py
+++ b/solution.py
@@ -17,8 +17,6 @@
 
 def mirror(greater):
     count = lax.axis_size("space")
-    forward = [(i, i + 1) for i in range(count - 1)]
-    backward = [(i + 1, i) for i in range(count - 1)]
     below = lax.ppermute(greater[2], "space", forward)
     above = lax.ppermute(greater[0], "space", backward)
     return flip_tiles(jnp.stack([below, greater[1], above]))
@@ -84,8 +82,6 @@
 def on_device(lesser, greater):
     count = lax.axis_size("space")
     total = lax.axis_size("energy")
-    forward = [(i, i + 1) for i in range(count - 1)]
-    backward = [(i + 1, i) for i in range(count - 1)]
     tiles, height, width = lesser.shape[2:]
     rows = tiles * height // total
     if rows % 16 == 0 and height % 16 == 0:
@@ -95,8 +91,13 @@
     got = lax.all_to_all(both, "energy", split_axis=0, concat_axis=0, tiled=True)
     left = got[:, 0]
     mine = got[:, 1]
-    below = lax.ppermute(mine, "space", forward)
-    above = lax.ppermute(mine, "space", backward)
+    inner = [(i, i ^ 1) for i in range(count) if i ^ 1 < count]
+    outer = [(i, j) for i in range(1, count) for j in (i - 1, i + 1) if (i % 2 == 1) == (j == i + 1) and 0 <= j < count]
+    near = lax.ppermute(mine, "space", inner)
+    far = lax.ppermute(mine, "space", outer)
+    odd = lax.axis_index("space") % 2 == 1
+    below = jnp.where(odd, near, far)
+    above = jnp.where(odd, far, near)
     first = lax.axis_index("energy") * rows
     tile = (first + lax.broadcasted_iota(jnp.int32, (1, rows, 1), 1)) // height
     right = jnp.where(tile == 0, below, jnp.where(tile == 1, mine, above))

time: 44.3 us -> 43.5 us (0.982)
  starting transfers between devices: 14.8 us -> 12.9 us
  waiting for transfers between devices: 11.7 us -> 12.4 us
  blocking collectives: 14 us -> 14.5 us
    ppermute x2, starting transfers between devices: 8.41 us -> 6.56 us  [the longest x1 6.49 us: on_device(): far = lax.ppermute(mine, 'space', outer)]
    ppermute x2, waiting for transfers between devices: 2.56 us -> 3.23 us  [the longest x1 3.22 us: on_device(): far = lax.ppermute(mine, 'space', outer)]
    all_to_all x1, blocking collectives: 14 us -> 14.5 us  [on_device(): lax.all_to_all(summed, 'energy', split_axis=0, concat_axis=0, tiled=True)]
  transfers between devices with their start and end apart: 3 -> 3, of which waited for: 3 -> 2; matrix products, arithmetic and copies ran while one was open for 0% -> 0% of each run, Pallas kernels for 0% -> 0%
where the time goes in v5:
time: 43.5 us; the launch traced here: 43.3 us
  blocking collectives  14.5 us (33%)
  starting transfers between devices  12.9 us (30%)
  waiting for transfers between devices  12.4 us (29%)
  Pallas kernels  1.9 us (4%)
  local copies, waits for them, and re-layouts  0.77 us (2%)
  other arithmetic  0.64 us (1%)
    all_to_all x1, blocking collectives, on_device(): lax.all_to_all(summed, 'energy', split_axis=0, concat_axis=0, tiled=True)  14.5 us
    all_to_all x1, waiting for transfers between devices, on_device(): lax.all_to_all(both, 'energy', split_axis=0, concat_axis=0, tiled=True)  9.16 us
    ppermute x1, starting transfers between devices, on_device(): far = lax.ppermute(mine, 'space', outer)  6.49 us
    all_to_all x1, starting transfers between devices, on_device(): lax.all_to_all(both, 'energy', split_axis=0, concat_axis=0, tiled=True)  6.34 us
    ppermute x1, waiting for transfers between devices, on_device(): far = lax.ppermute(mine, 'space', outer)  3.22 us
    pallas_call x1, Pallas kernels, pack(): pl.pallas_call(functools.partial(pack_kernel, total, rows), out_shape=jax...  1.9 us
  transfers between devices with their start and end apart: 3, of which 2 were waited for; matrix products, arithmetic and copies ran while one was open for 0% of the time, Pallas kernels for 0%

profile of v5, /device:TPU:1, one launch (start us, length us, event | category | flops | bytes accessed | tf_op | source)
XLA Modules:
  0.0 43.3 jit_solution(2177706021421014967)
XLA Ops:
  0.0 1.9 %shard_map.28 = bf16[8,2,48,256]{3,2,1,0:T(8,128)(2,1)} custom-call(bf16[3,128,256]{2,1,0:T(8,128)(2,1)} %bitcast.47, bf16[3,128,256]{2,1,0:T(8,128)(2,1)} %bitcast.48), custom_call_target="tpu_custom_call" | custom-call | bytes 786432 | tf_op jit(solution)/shard_map/pallas_call | solution.py:66
  1.9 6.3 %all-to-all-start = ((bf16[8,2,48,256]{3,2,1,0:T(8,128)(2,1)}), bf16[8,2,48,256]{3,2,1,0:T(8,128)(2,1)S(1)}, u32[]{:S(2)}, u32[]{:S(2)}) async-start(bf16[8,2,48,256]{3,2,1,0:T(8,128)(2,1)} %shard_map.28), calls=%async_computation | async-start | bytes 786432 | tf_op jit(solution)/shard_map/all_to_all | solution.py:91
  8.3 9.2 %all-to-all-done = bf16[8,2,48,256]{3,2,1,0:T(8,128)(2,1)S(1)} async-done(((bf16[8,2,48,256]{3,2,1,0:T(8,128)(2,1)}), bf16[8,2,48,256]{3,2,1,0:T(8,128)(2,1)S(1)}, u32[]{:S(2)}, u32[]{:S(2)}) %all-to-all-start) | async-done | bytes 393248 | tf_op jit(solution)/shard_map/all_to_all | solution.py:91
  17.5 6.5 %collective-permute-start.1 = (bf16[8,48,256]{2,1,0:T(8,128)(2,1)S(1)}, bf16[8,48,256]{2,1,0:T(8,128)(2,1)S(1)}, u32[]{:S(2)}, u32[]{:S(2)}) collective-permute-start(bf16[8,48,256]{2,1,0:T(8,128)(2,1)S(1)} %get-tuple-element.26), channel_id=1, source_target_pairs={{8,16},{16,8},{9,17},{17,9},{10,18},{18,10},{11,19},{19,11},{12,20... | collective-permute-start | bytes 589832 | tf_op jit(solution)/shard_map/ppermute | solution.py:97
  24.0 0.1 collective-permute-start
  24.1 3.2 %collective-permute-done.1 = bf16[8,48,256]{2,1,0:T(8,128)(2,1)S(1)} collective-permute-done((bf16[8,48,256]{2,1,0:T(8,128)(2,1)S(1)}, bf16[8,48,256]{2,1,0:T(8,128)(2,1)S(1)}, u32[]{:S(2)}, u32[]{:S(2)}) %collective-permute-start.1) | collective-permute-done | bytes 196640 | tf_op jit(solution)/shard_map/ppermute | solution.py:97
  27.3 0.0 collective-permute-done
  27.3 0.1 select_convert_fusion
  27.4 0.1 subtract_reduce_fusion.2
  27.5 0.1 subtract_reduce_fusion.1
  27.6 0.1 subtract_reduce_fusion
  27.7 0.1 add_reduce_fusion.1
  27.8 0.1 add_reduce_fusion
  28.0 14.5 %all_to_all.10 = f32[8,48,256]{2,1,0:T(8,128)S(1)} all-to-all(f32[8,48,256]{2,1,0:T(8,128)S(1)} %fusion.20), channel_id=1, replica_groups=mesh['space'=4,'energy'=8] {'energy'}, dimensions={0} | all-to-all | bytes 786432 | tf_op jit(solution)/shard_map/all_to_all | solution.py:105
  42.5 0.7 %copy.13 = f32[1,1,3,128,256]{4,3,2,1,0:T(8,128)} copy(f32[1,1,3,128,256]{4,3,2,1,0:T(8,128)S(1)} %bitcast.46) | data formatting | bytes 786432
  (11 shorter events, 0.1 us)
Async XLA Ops:
  1.9 15.5 %all-to-all-start = ((bf16[8,2,48,256]{3,2,1,0:T(8,128)(2,1)}), bf16[8,2,48,256]{3,2,1,0:T(8,128)(2,1)S(1)}, u32[]{:S(2)}, u32[]{:S(2)}) async-start(bf16[8,2,48,256]{3,2,1,0:T(8,128)(2,1)} %shard_map.28), calls=%async_computation | async-start | bytes 786432 | tf_op jit(solution)/shard_map/all_to_all | solution.py:91
  17.5 9.8 %collective-permute-start.1 = (bf16[8,48,256]{2,1,0:T(8,128)(2,1)S(1)}, bf16[8,48,256]{2,1,0:T(8,128)(2,1)S(1)}, u32[]{:S(2)}, u32[]{:S(2)}) collective-permute-start(bf16[8,48,256]{2,1,0:T(8,128)(2,1)S(1)} %get-tuple-element.26), channel_id=1, source_target_pairs={{8,16},{16,8},{9,17},{17,9},{10,18},{18,10},{11,19},{19,11},{12,20... | collective-permute-start | bytes 589832 | tf_op jit(solution)/shard_map/ppermute | solution.py:97
  24.0 3.3 %collective-permute-start = (bf16[8,48,256]{2,1,0:T(8,128)(2,1)S(1)}, bf16[8,48,256]{2,1,0:T(8,128)(2,1)S(1)}, u32[]{:S(2)}, u32[]{:S(2)}) collective-permute-start(bf16[8,48,256]{2,1,0:T(8,128)(2,1)S(1)} %get-tuple-element.26), channel_id=1, source_target_pairs={{0,8},{8,0},{16,24},{24,16},{1,9},{9,1},{17,25},{25,17},{2,10},{10... | collective-permute-start | bytes 589832 | tf_op jit(solution)/shard_map/ppermute | solution.py:96

commit v6 on v5

--- a/solution.py
+++ b/solution.py
@@ -13,13 +13,6 @@
     split = tiles.reshape(shape[:-1] + (2, width))
     turned = jnp.swapaxes(split, -3, -1)
     return turned.reshape(shape)
-
-
-def mirror(greater):
-    count = lax.axis_size("space")
-    below = lax.ppermute(greater[2], "space", forward)
-    above = lax.ppermute(greater[0], "space", backward)
-    return flip_tiles(jnp.stack([below, greater[1], above]))
 
 
 def correlate(left, right):

time: 43.5 us -> 43.5 us (level)
  no operation moved by 1% of the time
where the time goes in v6:
time: 43.5 us; the launch traced here: 43.3 us
  blocking collectives  14.5 us (33%)
  starting transfers between devices  12.9 us (30%)
  waiting for transfers between devices  12.4 us (29%)
  Pallas kernels  1.9 us (4%)
  local copies, waits for them, and re-layouts  0.77 us (2%)
  other arithmetic  0.64 us (1%)
    all_to_all x1, blocking collectives, on_device(): lax.all_to_all(summed, 'energy', split_axis=0, concat_axis=0, tiled=True)  14.5 us
    all_to_all x1, waiting for transfers between devices, on_device(): lax.all_to_all(both, 'energy', split_axis=0, concat_axis=0, tiled=True)  9.16 us
    ppermute x1, starting transfers between devices, on_device(): far = lax.ppermute(mine, 'space', outer)  6.49 us
    all_to_all x1, starting transfers between devices, on_device(): lax.all_to_all(both, 'energy', split_axis=0, concat_axis=0, tiled=True)  6.34 us
    ppermute x1, waiting for transfers between devices, on_device(): far = lax.ppermute(mine, 'space', outer)  3.22 us
    pallas_call x1, Pallas kernels, pack(): pl.pallas_call(functools.partial(pack_kernel, total, rows), out_shape=jax...  1.9 us
  transfers between devices with their start and end apart: 3, of which 2 were waited for; matrix products, arithmetic and copies ran while one was open for 0% of the time, Pallas kernels for 0%

profile of v6, /device:TPU:1, one launch (start us, length us, event | category | flops | bytes accessed | tf_op | source)
XLA Modules:
  0.0 43.3 jit_solution(2177706021421014967)
XLA Ops:
  0.0 1.9 %shard_map.28 = bf16[8,2,48,256]{3,2,1,0:T(8,128)(2,1)} custom-call(bf16[3,128,256]{2,1,0:T(8,128)(2,1)} %bitcast.47, bf16[3,128,256]{2,1,0:T(8,128)(2,1)} %bitcast.48), custom_call_target="tpu_custom_call" | custom-call | bytes 786432 | tf_op jit(solution)/shard_map/pallas_call | solution.py:59
  1.9 6.3 %all-to-all-start = ((bf16[8,2,48,256]{3,2,1,0:T(8,128)(2,1)}), bf16[8,2,48,256]{3,2,1,0:T(8,128)(2,1)S(1)}, u32[]{:S(2)}, u32[]{:S(2)}) async-start(bf16[8,2,48,256]{3,2,1,0:T(8,128)(2,1)} %shard_map.28), calls=%async_computation | async-start | bytes 786432 | tf_op jit(solution)/shard_map/all_to_all | solution.py:84
  8.3 9.2 %all-to-all-done = bf16[8,2,48,256]{3,2,1,0:T(8,128)(2,1)S(1)} async-done(((bf16[8,2,48,256]{3,2,1,0:T(8,128)(2,1)}), bf16[8,2,48,256]{3,2,1,0:T(8,128)(2,1)S(1)}, u32[]{:S(2)}, u32[]{:S(2)}) %all-to-all-start) | async-done | bytes 393248 | tf_op jit(solution)/shard_map/all_to_all | solution.py:84
  17.5 6.5 %collective-permute-start.1 = (bf16[8,48,256]{2,1,0:T(8,128)(2,1)S(1)}, bf16[8,48,256]{2,1,0:T(8,128)(2,1)S(1)}, u32[]{:S(2)}, u32[]{:S(2)}) collective-permute-start(bf16[8,48,256]{2,1,0:T(8,128)(2,1)S(1)} %get-tuple-element.26), channel_id=1, source_target_pairs={{8,16},{16,8},{9,17},{17,9},{10,18},{18,10},{11,19},{19,11},{12,20... | collective-permute-start | bytes 589832 | tf_op jit(solution)/shard_map/ppermute | solution.py:90
  24.0 0.1 collective-permute-start
  24.1 3.2 %collective-permute-done.1 = bf16[8,48,256]{2,1,0:T(8,128)(2,1)S(1)} collective-permute-done((bf16[8,48,256]{2,1,0:T(8,128)(2,1)S(1)}, bf16[8,48,256]{2,1,0:T(8,128)(2,1)S(1)}, u32[]{:S(2)}, u32[]{:S(2)}) %collective-permute-start.1) | collective-permute-done | bytes 196640 | tf_op jit(solution)/shard_map/ppermute | solution.py:90
  27.3 0.0 collective-permute-done
  27.3 0.1 select_convert_fusion
  27.4 0.1 subtract_reduce_fusion.2
  27.5 0.1 subtract_reduce_fusion.1
  27.6 0.1 subtract_reduce_fusion
  27.7 0.1 add_reduce_fusion.1
  27.8 0.1 add_reduce_fusion
  28.0 14.5 %all_to_all.10 = f32[8,48,256]{2,1,0:T(8,128)S(1)} all-to-all(f32[8,48,256]{2,1,0:T(8,128)S(1)} %fusion.20), channel_id=1, replica_groups=mesh['space'=4,'energy'=8] {'energy'}, dimensions={0} | all-to-all | bytes 786432 | tf_op jit(solution)/shard_map/all_to_all | solution.py:98
  42.5 0.7 %copy.13 = f32[1,1,3,128,256]{4,3,2,1,0:T(8,128)} copy(f32[1,1,3,128,256]{4,3,2,1,0:T(8,128)S(1)} %bitcast.46) | data formatting | bytes 786432
  (11 shorter events, 0.1 us)
Async XLA Ops:
  1.9 15.5 %all-to-all-start = ((bf16[8,2,48,256]{3,2,1,0:T(8,128)(2,1)}), bf16[8,2,48,256]{3,2,1,0:T(8,128)(2,1)S(1)}, u32[]{:S(2)}, u32[]{:S(2)}) async-start(bf16[8,2,48,256]{3,2,1,0:T(8,128)(2,1)} %shard_map.28), calls=%async_computation | async-start | bytes 786432 | tf_op jit(solution)/shard_map/all_to_all | solution.py:84
  17.5 9.8 %collective-permute-start.1 = (bf16[8,48,256]{2,1,0:T(8,128)(2,1)S(1)}, bf16[8,48,256]{2,1,0:T(8,128)(2,1)S(1)}, u32[]{:S(2)}, u32[]{:S(2)}) collective-permute-start(bf16[8,48,256]{2,1,0:T(8,128)(2,1)S(1)} %get-tuple-element.26), channel_id=1, source_target_pairs={{8,16},{16,8},{9,17},{17,9},{10,18},{18,10},{11,19},{19,11},{12,20... | collective-permute-start | bytes 589832 | tf_op jit(solution)/shard_map/ppermute | solution.py:90
  24.0 3.3 %collective-permute-start = (bf16[8,48,256]{2,1,0:T(8,128)(2,1)S(1)}, bf16[8,48,256]{2,1,0:T(8,128)(2,1)S(1)}, u32[]{:S(2)}, u32[]{:S(2)}) collective-permute-start(bf16[8,48,256]{2,1,0:T(8,128)(2,1)S(1)} %get-tuple-element.26), channel_id=1, source_target_pairs={{0,8},{8,0},{16,24},{24,16},{1,9},{9,1},{17,25},{25,17},{2,10},{10... | collective-permute-start | bytes 589832 | tf_op jit(solution)/shard_map/ppermute | solution.py:89

commit v7 on v6

v7 whole, which is shorter than its diff:
```python
import functools
import jax
import jax.numpy as jnp
from jax import lax
from jax.experimental import pallas as pl
from jax.experimental.pallas import tpu as pltpu
from jax.sharding import PartitionSpec as P


def flip_tiles(tiles):
    shape = tiles.shape
    width = shape[-2]
    split = tiles.reshape(shape[:-1] + (2, width))
    turned = jnp.swapaxes(split, -3, -1)
    return turned.reshape(shape)


def correlate(left, right):
    total = left.shape[0]
    width = left.shape[-1] // 2
    left = left.astype(jnp.float32)
    right = right.astype(jnp.float32)
    lre = jnp.concatenate([left[..., :width]] * 2)
    lim = jnp.concatenate([left[..., width:]] * 2)
    rre = right[..., :width]
    rim = right[..., width:]
    outs = []
    for shift in range(total):
        a = lre[shift:shift + total]
        b = lim[shift:shift + total]
        pre = jnp.sum(a * rre - b * rim, axis=0)
        pim = jnp.sum(a * rim + b * rre, axis=0)
        outs.append(jnp.concatenate([pre, pim], axis=-1))
    return jnp.stack(outs)


def pack_kernel(total, rows, lesser_ref, greater_ref, out_ref):
    tiles, height, width = lesser_ref.shape
    half = width // 2
    for tile in range(tiles):
        blocks = [greater_ref[tile, :, part * half:(part + 1) * half].T for part in range(2)]
        for chunk in range(total):
            span = slice(chunk * rows, (chunk + 1) * rows)
            out_ref[chunk, 0, tile] = lesser_ref[tile, span, :]
            for part in range(2):
                out_ref[chunk, 1, tile, :, part * half:(part + 1) * half] = blocks[part][span]


def pack(lesser, greater, total, rows):
    tiles, height, width = lesser.shape
    return pl.pallas_call(
        functools.partial(pack_kernel, total, rows),
        out_shape=jax.ShapeDtypeStruct((total, 2, tiles, rows, width), lesser.dtype),
        in_specs=[pl.BlockSpec(memory_space=pltpu.VMEM)] * 2,
        out_specs=pl.BlockSpec(memory_space=pltpu.VMEM),
        cost_estimate=pl.CostEstimate(flops=0, transcendentals=0, bytes_accessed=4 * lesser.size * 2),
    )(lesser, greater)


def pack_plain(lesser, greater, total, rows):
    tiles, height, width = lesser.shape
    both = jnp.stack([lesser, flip_tiles(greater)])
    return jnp.swapaxes(both.reshape(2, tiles, total, rows, width), 0, 2).swapaxes(1, 2)


def on_device(lesser, greater):
    count = lax.axis_size("space")
    total = lax.axis_size("energy")
    tiles, height, width = lesser.shape[2:]
    rows = height // total
    if rows % 16 == 0:
        both = pack(lesser[0, 0], greater[0, 0], total, rows)
    else:
        both = pack_plain(lesser[0, 0], greater[0, 0], total, rows)
    got = lax.all_to_all(both, "energy", split_axis=0, concat_axis=0, tiled=True)
    left = got[:, 0]
    turned = got[:, 1]
    odd = lax.axis_index("space") % 2 == 1
    inner = [(i, i ^ 1) for i in range(count) if i ^ 1 < count]
    outer = [(i, j) for i in range(1, count) for j in (i - 1, i + 1) if (i % 2 == 1) == (j == i + 1) and 0 <= j < count]
    near = lax.ppermute(jnp.where(odd, turned[:, 0], turned[:, 2]), "space", inner)
    far = lax.ppermute(jnp.where(odd, turned[:, 2], turned[:, 0]), "space", outer)
    below = jnp.where(odd, near, far)
    above = jnp.where(odd, far, near)
    right = jnp.stack([below, turned[:, 1], above], axis=1)
    summed = correlate(left, right)
    back = lax.all_to_all(summed, "energy", split_axis=0, concat_axis=0, tiled=True)
    return jnp.swapaxes(back, 0, 1).reshape((1, 1, tiles, height, width))


def solution(mesh):
    return jax.shard_map(
        on_device,
        mesh=mesh,
        in_specs=(P("energy", "space", None, None, None), P("energy", "space", None, None, None)),
        out_specs=P("energy", "space", None, None, None),
        check_vma=False,
    )
```

time: 43.5 us -> 40.1 us (0.922)
  blocking collectives: 14.5 us -> 11.9 us
  waiting for transfers between devices: 12.4 us -> 11.6 us
    all_to_all x1, blocking collectives: 14.5 us -> 11.9 us  [on_device(): lax.all_to_all(summed, 'energy', split_axis=0, concat_axis=0, tiled=True)]
    all_to_all x0 -> x1, local copies, waits for them, and re-layouts: none -> 0.77 us  [on_device(): lax.all_to_all(summed, 'energy', split_axis=0, concat_axis=0, tiled=True)]
    ppermute x2, waiting for transfers between devices: 3.23 us -> 2.46 us  [the longest x1 2.46 us: on_device(): lax.ppermute(jnp.where(odd, turned[:, 2], turned[:, 0]), 'space', outer)]
    unnamed x1 -> x0, local copies, waits for them, and re-layouts: 0.75 us -> none
where the time goes in v7:
time: 40.1 us; the launch traced here: 39.9 us
  starting transfers between devices  12.9 us (32%)
  blocking collectives  11.9 us (30%)
  waiting for transfers between devices  11.6 us (29%)
  Pallas kernels  1.87 us (5%)
  local copies, waits for them, and re-layouts  0.81 us (2%)
  other arithmetic  0.58 us (1%)
    all_to_all x1, blocking collectives, on_device(): lax.all_to_all(summed, 'energy', split_axis=0, concat_axis=0, tiled=True)  11.9 us
    all_to_all x1, waiting for transfers between devices, on_device(): lax.all_to_all(both, 'energy', split_axis=0, concat_axis=0, tiled=True)  9.17 us
    all_to_all x1, starting transfers between devices, on_device(): lax.all_to_all(both, 'energy', split_axis=0, concat_axis=0, tiled=True)  6.34 us
    ppermute x1, starting transfers between devices, on_device(): lax.ppermute(jnp.where(odd, turned[:, 0], turned[:, 2]), 'space', inner)  3.52 us
    ppermute x1, starting transfers between devices, on_device(): lax.ppermute(jnp.where(odd, turned[:, 2], turned[:, 0]), 'space', outer)  3.05 us
    ppermute x1, waiting for transfers between devices, on_device(): lax.ppermute(jnp.where(odd, turned[:, 2], turned[:, 0]), 'space', outer)  2.46 us
    pallas_call x1, Pallas kernels, pack(): pl.pallas_call(functools.partial(pack_kernel, total, rows), out_shape=jax...  1.87 us
  transfers between devices with their start and end apart: 3, of which 2 were waited for; matrix products, arithmetic and copies ran while one was open for 0% of the time, Pallas kernels for 0%

profile of v7, /device:TPU:1, one launch (start us, length us, event | category | flops | bytes accessed | tf_op | source)
XLA Modules:
  0.0 39.9 jit_solution(3408413185094661540)
XLA Ops:
  0.0 1.9 %shard_map.28 = bf16[8,2,3,16,256]{4,3,2,1,0:T(8,128)(2,1)} custom-call(bf16[3,128,256]{2,1,0:T(8,128)(2,1)} %bitcast.68, bf16[3,128,256]{2,1,0:T(8,128)(2,1)} %bitcast.69), custom_call_target="tpu_custom_call" | custom-call | bytes 786432 | tf_op jit(solution)/shard_map/pallas_call | solution.py:51
  1.9 6.3 %all-to-all-start = ((bf16[8,2,3,16,256]{4,3,2,1,0:T(8,128)(2,1)}), bf16[8,2,3,16,256]{4,3,2,1,0:T(8,128)(2,1)S(1)}, u32[]{:S(2)}, u32[]{:S(2)}) async-start(bf16[8,2,3,16,256]{4,3,2,1,0:T(8,128)(2,1)} %shard_map.28), calls=%async_computation | async-start | bytes 786432 | tf_op jit(solution)/shard_map/all_to_all | solution.py:75
  8.2 9.2 %all-to-all-done = bf16[8,2,3,16,256]{4,3,2,1,0:T(8,128)(2,1)S(1)} async-done(((bf16[8,2,3,16,256]{4,3,2,1,0:T(8,128)(2,1)}), bf16[8,2,3,16,256]{4,3,2,1,0:T(8,128)(2,1)S(1)}, u32[]{:S(2)}, u32[]{:S(2)}) %all-to-all-start) | async-done | bytes 393248 | tf_op jit(solution)/shard_map/all_to_all | solution.py:75
  17.5 3.5 %collective-permute-start = (bf16[8,16,256]{2,1,0:T(8,128)(2,1)S(1)}, bf16[8,16,256]{2,1,0:T(8,128)(2,1)S(1)}, u32[]{:S(2)}, u32[]{:S(2)}) collective-permute-start(bf16[8,16,256]{2,1,0:T(8,128)(2,1)S(1)} %get-tuple-element.27), channel_id=1, source_target_pairs={{0,8},{8,0},{16,24},{24,16},{1,9},{9,1},{17,25},{25,17},{2,10},{10... | collective-permute-start | bytes 196616 | tf_op jit(solution)/shard_map/ppermute | solution.py:81
  21.0 3.0 %collective-permute-start.1 = (bf16[8,16,256]{2,1,0:T(8,128)(2,1)S(1)}, bf16[8,16,256]{2,1,0:T(8,128)(2,1)S(1)}, u32[]{:S(2)}, u32[]{:S(2)}) collective-permute-start(bf16[8,16,256]{2,1,0:T(8,128)(2,1)S(1)} %get-tuple-element.28), channel_id=1, source_target_pairs={{8,16},{16,8},{9,17},{17,9},{10,18},{18,10},{11,19},{19,11},{12,20... | collective-permute-start | bytes 196616 | tf_op jit(solution)/shard_map/ppermute | solution.py:82
  24.1 0.0 collective-permute-done
  24.1 2.5 %collective-permute-done.1 = bf16[8,16,256]{2,1,0:T(8,128)(2,1)S(1)} collective-permute-done((bf16[8,16,256]{2,1,0:T(8,128)(2,1)S(1)}, bf16[8,16,256]{2,1,0:T(8,128)(2,1)S(1)}, u32[]{:S(2)}, u32[]{:S(2)}) %collective-permute-start.1) | collective-permute-done | bytes 65568 | tf_op jit(solution)/shard_map/ppermute | solution.py:82
  26.6 0.1 subtract_reduce_fusion.2
  26.7 0.1 subtract_reduce_fusion.1
  26.8 0.1 subtract_reduce_fusion
  26.9 0.1 add_reduce_fusion.1
  27.0 0.1 add_reduce_fusion
  27.2 11.9 %all_to_all.10 = f32[8,3,16,256]{3,2,1,0:T(8,128)S(1)} all-to-all(f32[8,3,16,256]{3,2,1,0:T(8,128)S(1)} %fusion.20), channel_id=1, replica_groups=mesh['space'=4,'energy'=8] {'energy'}, dimensions={0} | all-to-all | bytes 786432 | tf_op jit(solution)/shard_map/all_to_all | solution.py:87
  39.1 0.8 %copy.15 = f32[8,3,16,256]{3,2,0,1:T(8,128)} copy(f32[8,3,16,256]{3,2,1,0:T(8,128)S(1)} %all_to_all.10) | data formatting | bytes 786432 | tf_op jit(solution)/shard_map/all_to_all | solution.py:87
  (14 shorter events, 0.2 us)
Async XLA Ops:
  1.9 15.5 %all-to-all-start = ((bf16[8,2,3,16,256]{4,3,2,1,0:T(8,128)(2,1)}), bf16[8,2,3,16,256]{4,3,2,1,0:T(8,128)(2,1)S(1)}, u32[]{:S(2)}, u32[]{:S(2)}) async-start(bf16[8,2,3,16,256]{4,3,2,1,0:T(8,128)(2,1)} %shard_map.28), calls=%async_computation | async-start | bytes 786432 | tf_op jit(solution)/shard_map/all_to_all | solution.py:75
  17.5 6.6 %collective-permute-start = (bf16[8,16,256]{2,1,0:T(8,128)(2,1)S(1)}, bf16[8,16,256]{2,1,0:T(8,128)(2,1)S(1)}, u32[]{:S(2)}, u32[]{:S(2)}) collective-permute-start(bf16[8,16,256]{2,1,0:T(8,128)(2,1)S(1)} %get-tuple-element.27), channel_id=1, source_target_pairs={{0,8},{8,0},{16,24},{24,16},{1,9},{9,1},{17,25},{25,17},{2,10},{10... | collective-permute-start | bytes 196616 | tf_op jit(solution)/shard_map/ppermute | solution.py:81
  21.0 5.6 %collective-permute-start.1 = (bf16[8,16,256]{2,1,0:T(8,128)(2,1)S(1)}, bf16[8,16,256]{2,1,0:T(8,128)(2,1)S(1)}, u32[]{:S(2)}, u32[]{:S(2)}) collective-permute-start(bf16[8,16,256]{2,1,0:T(8,128)(2,1)S(1)} %get-tuple-element.28), channel_id=1, source_target_pairs={{8,16},{16,8},{9,17},{17,9},{10,18},{18,10},{11,19},{19,11},{12,20... | collective-permute-start | bytes 196616 | tf_op jit(solution)/shard_map/ppermute | solution.py:82
